TPU v7x, 256 devices: a whole 4x4x8 slice. The times are simulated.
256 devices in a mesh: facet: 8 (over z), chan: 32 (over y, x, core).
Axes of the slice: x: 4, y: 4, z: 8, core: 2. Of those that a mesh axis runs over, the one named last changes fastest.
Arguments:
- sky_image: float32 [256, 32, 4096], P('chan', 'facet'), may hold values from -100 to 100
- dual_field: float32 [256, 32, 4096], P(None, 'facet', 'chan'), may hold values from -100 to 100
- sketch_matrix: bfloat16 [32, 4096, 128], P('facet', 'chan'), may hold values from -0.046875 to 0.046875
- grid_tiles: float32 [256, 4, 128, 128], P('chan'), may hold values from -0.5 to 0.5
- freq_block: int32 [256, 4], P('chan'), may hold values from 0 to 31
- vis_block: int32 [256, 4], P('chan'), may hold values from 0 to 3
- vis_data: float32 [256, 2, 32, 4, 128], P('chan', None, 'facet'), may hold values from -6 to 6
Outputs:
- new_image: float32 [256, 32, 4096], P('chan', 'facet')
- new_dual: float32 [256, 32, 4096], P(None, 'facet', 'chan')
All inputs are finite; a program needn't handle non-finite values.
Results may differ from a plain program's by a relative error of at most 0.0003.
Values sent between devices are 32-bit elements; how exact they have to be, the bound alone decides.
No kernel may reach another device: no remote copies, remote signals or barrier semaphores. Data moves between devices by JAX's collectives and lax.ppermute only.
A program may use at most 128 MiB of HBM per device.

v0:
```python
import math

import jax
import jax.numpy as jnp
from jax import lax
from jax.sharding import PartitionSpec as P

SIGN_ITERS = 12
ROOT_ITERS = 14


step_primal = 0.4
smooth_weight = 0.25
step_dual = 0.5
shrink_ratio = 0.25


def padded_2(block, sides, width):
    for axis, dim in sides:
        count = lax.axis_size(axis)
        forward = [(i, i + 1) for i in range(count - 1)]
        backward = [(target, source) for source, target in forward]
        low = lax.ppermute(
            lax.slice_in_dim(block, block.shape[dim] - width, None, axis=dim), axis, forward
        )
        high = lax.ppermute(lax.slice_in_dim(block, 0, width, axis=dim), axis, backward)
        block = jnp.concatenate([low, block, high], axis=dim)
    return block


def matmul_hi(first_mat, second_mat):
    return jnp.dot(first_mat, second_mat, precision=lax.Precision.HIGHEST)


def shrink_matrix(gram_mat):
    order_n = gram_mat.shape[0]
    identity = jnp.eye(order_n, dtype=gram_mat.dtype)
    thresh_sq = shrink_ratio * jnp.trace(gram_mat) / order_n
    shifted = gram_mat - thresh_sq * identity
    signum = shifted / jnp.sqrt(jnp.sum(shifted * shifted))

    def sign_step(turn_no, current):
        return 1.5 * current - 0.5 * matmul_hi(matmul_hi(current, current), current)

    signum = lax.fori_loop(0, SIGN_ITERS, sign_step, signum)
    keeper = 0.5 * (identity + signum)
    floored = 0.5 * (gram_mat + thresh_sq * identity + matmul_hi(shifted, signum))
    scale_c = jnp.sqrt(jnp.sum(floored * floored))

    def root_step(turn_no, state_pair):
        root_iter, inv_iter = state_pair
        step_mat = 0.5 * (3.0 * identity - matmul_hi(inv_iter, root_iter))
        return (matmul_hi(root_iter, step_mat), matmul_hi(step_mat, inv_iter))

    root_iter, inv_iter = lax.fori_loop(0, ROOT_ITERS, root_step, (floored / scale_c, identity))
    inv_root = inv_iter / jnp.sqrt(scale_c)
    return matmul_hi(keeper, identity - jnp.sqrt(thresh_sq) * inv_root)


def basis_from(sketch):
    lower_fac = jnp.linalg.cholesky(matmul_hi(sketch.T, sketch))
    return jax.scipy.linalg.solve_triangular(lower_fac, sketch.T, lower=True).T


def phase_pair(count_a, count_b, period):
    first_idx = lax.broadcasted_iota(jnp.int32, (count_a, count_b), 0)
    second_idx = lax.broadcasted_iota(jnp.int32, (count_a, count_b), 1)
    angle_grid = 2.0 * math.pi / period * (first_idx * second_idx % period).astype(jnp.float32)
    return (jnp.cos(angle_grid), jnp.sin(angle_grid))


def spectrum_tables(width, block):
    blocks_n = width // block
    cos_a, sin_a = phase_pair(blocks_n, blocks_n, blocks_n)
    cos_b, sin_b = phase_pair(block, block, block)
    cos_t, sin_t = phase_pair(blocks_n, block, width)
    return (cos_a, sin_a, cos_b, sin_b, cos_t, sin_t)


def forward_rows(rows_img, tables, block):
    cos_a, sin_a, cos_b, sin_b, cos_t, sin_t = tables
    row_count, width = rows_img.shape
    blocks_n = width // block
    hi = lax.Precision.HIGHEST
    blocks = rows_img.reshape(row_count, blocks_n, block)
    part_re = jnp.einsum("kn,bnm->bkm", cos_a, blocks, precision=hi)
    part_im = -jnp.einsum("kn,bnm->bkm", sin_a, blocks, precision=hi)
    turned_re = (part_re * cos_t + part_im * sin_t).reshape(-1, block)
    turned_im = (part_im * cos_t - part_re * sin_t).reshape(-1, block)
    ortho_scale = 1.0 / math.sqrt(width)
    spec_re = (matmul_hi(turned_re, cos_b) + matmul_hi(turned_im, sin_b)) * ortho_scale
    spec_im = (matmul_hi(turned_im, cos_b) - matmul_hi(turned_re, sin_b)) * ortho_scale
    return (
        spec_re.reshape(row_count, blocks_n, block),
        spec_im.reshape(row_count, blocks_n, block),
    )


def adjoint_rows(spec_re, spec_im, tables):
    cos_a, sin_a, cos_b, sin_b, cos_t, sin_t = tables
    row_count, blocks_n, block = spec_re.shape
    hi = lax.Precision.HIGHEST
    flat_re = spec_re.reshape(-1, block)
    flat_im = spec_im.reshape(-1, block)
    back_re = (matmul_hi(flat_re, cos_b) - matmul_hi(flat_im, sin_b)).reshape(
        row_count, blocks_n, block
    )
    back_im = (matmul_hi(flat_im, cos_b) + matmul_hi(flat_re, sin_b)).reshape(
        row_count, blocks_n, block
    )
    turn_re = back_re * cos_t - back_im * sin_t
    turn_im = back_re * sin_t + back_im * cos_t
    rows_out = jnp.einsum("kn,bkm->bnm", cos_a, turn_re, precision=hi) - jnp.einsum(
        "kn,bkm->bnm", sin_a, turn_im, precision=hi
    )
    width = blocks_n * block
    return rows_out.reshape(row_count, width) * (1.0 / math.sqrt(width))


def data_gradient(sky_image, grid_tiles, freq_block, vis_block, vis_data):
    chan_count, row_count, width = sky_image.shape
    block = grid_tiles.shape[2]
    blocks_n = width // block
    hi = lax.Precision.HIGHEST
    tables = spectrum_tables(width, block)
    columns = lax.all_to_all(sky_image, "facet", split_axis=2, concat_axis=1, tiled=True)
    all_rows = columns.shape[1]
    cos_c, sin_c = phase_pair(all_rows, all_rows, all_rows)
    column_scale = 1.0 / math.sqrt(all_rows)
    column_re = jnp.einsum("pq,cqn->cpn", cos_c, columns, precision=hi) * column_scale
    column_im = -jnp.einsum("pq,cqn->cpn", sin_c, columns, precision=hi) * column_scale
    column_spec = jnp.stack([column_re, column_im], 1)
    row_spec = lax.all_to_all(column_spec, "facet", split_axis=2, concat_axis=3, tiled=True)
    four_re, four_im = forward_rows(
        row_spec.reshape(chan_count * 2 * row_count, width), tables, block
    )
    four_re = four_re.reshape(chan_count, 2, row_count, blocks_n, block)
    four_im = four_im.reshape(chan_count, 2, row_count, blocks_n, block)
    spec_re = four_re[:, 0] - four_im[:, 1]
    spec_im = four_im[:, 0] + four_re[:, 1]
    spectra = jnp.stack([spec_re, spec_im], 1)
    pick_onehot = jax.nn.one_hot(freq_block, blocks_n, dtype=jnp.float32)
    place_onehot = jax.nn.one_hot(vis_block, vis_data.shape[3], dtype=jnp.float32)
    chosen = jnp.einsum("ctb,cxrbk->cxtrk", pick_onehot, spectra, precision=hi)
    products = jnp.einsum("cxtrk,ctkm->cxtrm", chosen, grid_tiles, precision=hi)
    predicted = jnp.einsum("ctv,cxtrm->cxrvm", place_onehot, products, precision=hi)
    residual = predicted - vis_data
    spread = jnp.einsum("ctv,cxrvm->cxtrm", place_onehot, residual, precision=hi)
    pulled = jnp.einsum("cxtrm,ctkm->cxtrk", spread, grid_tiles, precision=hi)
    back_spec = jnp.einsum("ctb,cxtrk->cxrbk", pick_onehot, pulled, precision=hi)
    back_re = back_spec[:, 0].reshape(-1, blocks_n, block)
    back_im = back_spec[:, 1].reshape(-1, blocks_n, block)
    inverted = adjoint_rows(
        jnp.concatenate([back_re, back_im], 0), jnp.concatenate([back_im, -back_re], 0), tables
    )
    inverted = jnp.swapaxes(inverted.reshape(2, chan_count, row_count, width), 0, 1)
    spatial = lax.all_to_all(inverted, "facet", split_axis=3, concat_axis=2, tiled=True)
    gradient_cols = (
        jnp.einsum("pq,cpn->cqn", cos_c, spatial[:, 0], precision=hi)
        - jnp.einsum("pq,cpn->cqn", sin_c, spatial[:, 1], precision=hi)
    ) * column_scale
    return lax.all_to_all(gradient_cols, "facet", split_axis=1, concat_axis=2, tiled=True)


def take_sketch(pixels, sketch_rows):
    return jnp.einsum("crw,rwk->ck", pixels, sketch_rows, precision=lax.Precision.HIGHEST)


def project_rows(basis_mat, pixels):
    return jnp.einsum("ck,crw->krw", basis_mat, pixels, precision=lax.Precision.HIGHEST)


def on_device(sky_image, dual_field, sketch_matrix, grid_tiles, freq_block, vis_block, vis_data):
    hi = lax.Precision.HIGHEST
    dual_chan = lax.all_to_all(dual_field, "chan", split_axis=0, concat_axis=2, tiled=True)
    padded = padded_2(sky_image, (("facet", 1),), 1)
    gradient = data_gradient(sky_image, grid_tiles, freq_block, vis_block, vis_data)
    smooth = 2.0 * sky_image - padded[:, :-2] - padded[:, 2:]
    new_image = sky_image - step_primal * (gradient + smooth_weight * smooth + dual_chan)
    merged = dual_chan + step_dual * (2.0 * new_image - sky_image)
    sketch_rows = sketch_matrix.astype(jnp.float32)
    pixels = lax.all_to_all(merged, "chan", split_axis=2, concat_axis=0, tiled=True)
    sketch = lax.psum(take_sketch(pixels, sketch_rows), "chan")
    basis_mat = basis_from(sketch)
    coords = project_rows(basis_mat, pixels)
    gram_mat = lax.psum(jnp.einsum("krw,jrw->kj", coords, coords, precision=hi), "chan")
    shrink = shrink_matrix(gram_mat)
    new_dual = pixels - jnp.einsum(
        "ck,krw->crw", matmul_hi(basis_mat, shrink), coords, precision=hi
    )
    return (new_image, new_dual)


def solution(mesh):
    placed = (
        P("chan", "facet", None),
        P(None, "facet", "chan"),
        P("facet", "chan", None),
        P("chan", None, None, None),
        P("chan", None),
        P("chan", None),
        P("chan", None, "facet", None, None),
    )
    return jax.shard_map(
        on_device,
        mesh=mesh,
        in_specs=placed,
        out_specs=(P("chan", "facet", None), P(None, "facet", "chan")),
        check_vma=False,
    )
```

profile of v0, /device:TPU:1, one launch (start us, length us, event | category | flops | bytes accessed | tf_op | source)
XLA Modules:
  0.0 629.0 jit_solution(11363027889808603613)
XLA Ops:
  7.2 6.9 %copy.95 = f32[8,4,4096]{0,1,2:T(4,128)} copy(f32[8,4,4096]{2,1,0:T(4,128)} %param.11) | data formatting | bytes 1048576 | tf_op args[0]
  14.1 11.4 %reshape.86 = f32[8,1,16384]{2,1,0:T(1,128)S(1)} reshape(f32[4096,4,8]{2,1,0:T(4,128)} %bitcast.218) | data formatting | bytes 1048576
  25.5 25.4 %all_to_all.105 = f32[8,1,16384]{2,1,0:T(1,128)S(1)} all-to-all(f32[8,1,16384]{2,1,0:T(1,128)S(1)} %reshape.86), channel_id=1, replica_groups=mesh['facet'=8,'chan'=32] {'facet'}, dimensions={0} | all-to-all | bytes 1048576 | tf_op jit(solution)/shard_map/all_to_all | solution.py:126
  51.4 1.9 reduce.6
  53.3 13.1 %reshape.87 = f32[4096,4,8]{2,1,0:T(4,128)} reshape(f32[8,16384]{1,0:T(8,128)S(1)} %reduce.6) | data formatting | bytes 1048576
  66.4 6.7 %copy.96 = f32[8,4,8,512]{3,1,2,0:T(4,128)S(1)} copy(f32[8,4,8,512]{0,1,3,2:T(4,128)} %bitcast.215) | data formatting | bytes 1048576 | tf_op jit(solution)/shard_map/all_to_all | solution.py:126
  74.8 1.6 copy.99
  76.4 3.7 all-to-all-start.1
  80.4 28.5 %all-to-all-done.1 = f32[8,2,32,512]{3,0,1,2:T(8,128)S(1)} async-done(((f32[8,2,32,512]{3,0,1,2:T(8,128)}), f32[8,2,32,512]{3,0,1,2:T(8,128)S(1)}, u32[]{:S(2)}, u32[]{:S(2)}) %all-to-all-start.1) | async-done | bytes 1048608 | tf_op jit(solution)/shard_map/all_to_all | solution.py:133
  109.0 1.6 copy.155
  110.5 1.3 reshape_reshape.9
  111.8 1.1 fusion.12
  112.9 1.3 multiply_subtract_fusion
  114.3 1.2 fusion.87
  115.5 1.2 fusion.85
  116.7 1.2 fusion.5
  117.9 1.2 fusion.4
  119.9 1.9 fusion.18
  122.5 3.8 fusion.21
  127.4 1.2 fusion.83
  128.6 1.2 fusion.81
  129.8 1.2 convolution_subtract_fusion.1
  131.1 1.2 convolution_add_fusion
  132.3 1.2 fusion.32
  133.5 1.2 fusion.11
  135.1 11.1 %copy.110 = f32[2,8,4,4096]{1,2,0,3:T(4,128)} copy(f32[2,8,4,4096]{3,2,1,0:T(4,128)S(1)} %mul.315) | data formatting | bytes 2097152 | tf_op jit(solution)/shard_map/mul | solution.py:117
  146.2 14.5 %bitcast_bitcast_fusion = f32[4096,2,4,8]{3,2,1,0:T(4,128)} fusion(f32[2,8,4,4096]{1,2,0,3:T(4,128)} %copy.110), kind=kLoop, calls=%fused_computation.239 | loop fusion | bytes 2097152
  160.7 21.3 %reshape.88 = f32[8,1,32768]{2,1,0:T(1,128)S(1)} reshape(f32[4096,2,4,8]{3,2,1,0:T(4,128)} %bitcast_bitcast_fusion) | data formatting | bytes 2097152
  182.0 30.5 %all_to_all.106 = f32[8,1,32768]{2,1,0:T(1,128)S(1)} all-to-all(f32[8,1,32768]{2,1,0:T(1,128)S(1)} %reshape.88), channel_id=1, replica_groups=mesh['facet'=8,'chan'=32] {'facet'}, dimensions={0} | all-to-all | bytes 2097152 | tf_op jit(solution)/shard_map/all_to_all | solution.py:157
  212.5 3.1 reduce.7
  215.7 25.6 %reshape.89 = f32[4096,2,4,8]{3,2,1,0:T(4,128)} reshape(f32[8,32768]{1,0:T(8,128)S(1)} %reduce.7) | data formatting | bytes 2097152
  241.3 13.2 %copy.111 = f32[8,2,4,8,512]{4,2,3,0,1:T(4,128)S(1)} copy(f32[8,2,4,8,512]{0,2,1,4,3:T(4,128)} %bitcast.214) | data formatting | bytes 2097152 | tf_op jit(solution)/shard_map/all_to_all | solution.py:157
  256.2 1.1 copy.112
  257.3 3.5 all-to-all-start.3
  261.1 16.0 %all-to-all-done.3 = f32[8,32,512]{2,0,1:T(8,128)S(1)} async-done(((f32[8,32,512]{2,0,1:T(8,128)}), f32[8,32,512]{2,0,1:T(8,128)S(1)}, u32[]{:S(2)}, u32[]{:S(2)}) %all-to-all-start.3) | async-done | bytes 524320 | tf_op jit(solution)/shard_map/all_to_all | solution.py:162
  277.2 9.2 %all-to-all-start.4 = ((f32[256,4,128]{2,1,0:T(4,128)}), f32[256,4,128]{2,1,0:T(4,128)S(1)}, u32[]{:S(2)}, u32[]{:S(2)}) async-start(f32[256,4,128]{2,1,0:T(4,128)} %param.12), calls=%async_computation.4 | async-start | bytes 1048576 | tf_op jit(solution)/shard_map/all_to_all | solution.py:175
  286.5 2.2 collective-permute-start
  288.7 1.3 collective-permute-start.1
  290.0 1.3 collective-permute-done
  291.3 3.8 collective-permute-done.1
  295.1 2.7 all-to-all-done.4
  298.3 5.9 copy.122
  304.2 11.4 %reshape.90 = f32[32,1,4096]{2,1,0:T(1,128)S(1)} reshape(f32[4096,4,8]{2,1,0:T(4,128)} %bitcast.216) | data formatting | bytes 1048576
  315.6 17.2 %all_to_all.107 = f32[32,1,4096]{2,1,0:T(1,128)S(1)} all-to-all(f32[32,1,4096]{2,1,0:T(1,128)S(1)} %reshape.90), channel_id=1, replica_groups=mesh['facet'=8,'chan'=32] {'chan'}, dimensions={0} | all-to-all | bytes 1048576 | tf_op jit(solution)/shard_map/all_to_all | solution.py:182
  332.8 1.9 reduce.8
  334.7 11.3 %reshape.91 = f32[4096,4,8]{2,1,0:T(4,128)} reshape(f32[32,4096]{1,0:T(8,128)S(1)} %reduce.8) | data formatting | bytes 1048576
  346.0 6.7 %copy.123 = f32[8,4,32,128]{3,0,2,1:T(8,128)S(1)} copy(f32[8,4,32,128]{0,1,3,2:T(4,128)} %bitcast.217) | data formatting | bytes 1048576 | tf_op jit(solution)/shard_map/all_to_all | solution.py:182
  352.8 1.0 convolution_bitcast_fusion.3
  353.9 105.1 %all-reduce.3.cloned.1.call-done = f32[256,128]{1,0:T(8,128)} async-done(((f32[256,128]{1,0:T(8,128)}), f32[256,128]{1,0:T(8,128)}) %all-reduce.3.cloned.1.call-update) | async-done | bytes 131088 | tf_op jit(solution)/shard_map/psum | solution.py:183
  458.9 1.4 fusion.208
  460.4 11.7 %cholesky.22 = f32[128,128]{1,0:T(8,128)S(1)} custom-call(f32[128,128]{1,0:T(8,128)S(1)} %fusion.62), custom_call_target="Cholesky" | custom-call | tf_op jit(solution)/shard_map/jit(cholesky)/cholesky | solution.py:61
  473.5 9.8 %custom-call.7 = f32[1,128,128]{1,2,0:T(8,128)S(1)} custom-call(f32[1,128,128]{2,1,0:T(8,128)S(1)} %fusion.56), custom_call_target="InvertDiagBlocksLowerTriangular" | custom-call | tf_op jit(solution)/shard_map/jit(_solve_triangular)/triangular_solve | solution.py:62
  483.3 1.2 fusion.60
  485.0 1.0 convolution_bitcast_fusion.8
  486.0 1.1 copy.126
  487.1 106.4 %all-reduce.5.cloned.1.call-done = f32[128,128]{1,0:T(8,128)} async-done(((f32[128,128]{1,0:T(8,128)}), f32[128,128]{1,0:T(8,128)}) %all-reduce.5.cloned.1.call-update) | async-done | bytes 65552 | tf_op jit(solution)/shard_map/psum | solution.py:186
  593.5 1.5 select_reduce_fusion
  595.8 1.5 multiply_reduce_fusion.1
  598.1 0.9 fusion.70
  598.9 5.4 while.23
  604.4 1.8 multiply_reduce_fusion
  607.1 11.4 %while.24 = (s32[]{:T(128)}, f32[128,128]{0,1:T(8,128)S(1)}, f32[128,128]{1,0:T(8,128)S(1)}, s32[]{:T(128)}) while((s32[]{:T(128)}, f32[128,128]{0,1:T(8,128)S(1)}, f32[128,128]{1,0:T(8,128)S(1)}, s32[]{:T(128)}) %tuple.57), condition=%wide.region_10.11_spmd.clone, body=%wide.region_9.10_spmd.clone.sunk | while | flops 75563008 | bytes 852021 | solution.py:55
  618.7 1.3 convolution_bitcast_fusion.5
  620.6 1.1 copy.127
  (161 shorter events, 26.5 us)
Async XLA Ops:
  7.2 112.7 %copy-start = (f32[8,4,128,128]{3,2,1,0:T(8,128)S(1)}, f32[8,4,128,128]{3,2,1,0:T(8,128)}, u32[]{:S(2)}) copy-start(f32[8,4,128,128]{3,2,1,0:T(8,128)} %param.14) | copy-start | bytes 6291460
  66.4 13.8 %copy-start.6 = (s32[8,4]{0,1:T(4,128)S(1)}, s32[8,4]{0,1:T(4,128)}, u32[]{:S(2)}) copy-start(s32[8,4]{0,1:T(4,128)} %param.15) | copy-start | bytes 388
  66.4 13.9 %copy-start.7 = (s32[8,4]{0,1:T(4,128)S(1)}, s32[8,4]{0,1:T(4,128)}, u32[]{:S(2)}) copy-start(s32[8,4]{0,1:T(4,128)} %param.16) | copy-start | bytes 388
  76.4 32.5 %all-to-all-start.1 = ((f32[8,2,32,512]{3,0,1,2:T(8,128)}), f32[8,2,32,512]{3,0,1,2:T(8,128)S(1)}, u32[]{:S(2)}, u32[]{:S(2)}) async-start(f32[8,2,32,512]{3,0,1,2:T(8,128)} %copy.99), calls=%async_computation.1 | async-start | bytes 2097152 | tf_op jit(solution)/shard_map/all_to_all | solution.py:133
  114.2 7.5 %copy-start.4 = (f32[8,2,4,4,128]{4,3,2,1,0:T(4,128)S(1)}, f32[8,2,4,4,128]{4,3,2,1,0:T(4,128)}, u32[]{:S(2)}) copy-start(f32[8,2,4,4,128]{4,3,2,1,0:T(4,128)} %param.17) | copy-start | bytes 393220
  241.3 19.6 %copy-start.2 = (f32[8,4,4096]{2,1,0:T(4,128)S(1)}, f32[8,4,4096]{2,1,0:T(4,128)}, u32[]{:S(2)}) copy-start(f32[8,4,4096]{2,1,0:T(4,128)} %param.11) | copy-start | bytes 1572868
  257.3 19.9 %all-to-all-start.3 = ((f32[8,32,512]{2,0,1:T(8,128)}), f32[8,32,512]{2,0,1:T(8,128)S(1)}, u32[]{:S(2)}, u32[]{:S(2)}) async-start(f32[8,32,512]{2,0,1:T(8,128)} %copy.112), calls=%async_computation.3 | async-start | bytes 1048576 | tf_op jit(solution)/shard_map/all_to_all | solution.py:162
  277.2 20.7 %all-to-all-start.4 = ((f32[256,4,128]{2,1,0:T(4,128)}), f32[256,4,128]{2,1,0:T(4,128)S(1)}, u32[]{:S(2)}, u32[]{:S(2)}) async-start(f32[256,4,128]{2,1,0:T(4,128)} %param.12), calls=%async_computation.4 | async-start | bytes 1048576 | tf_op jit(solution)/shard_map/all_to_all | solution.py:175
  286.4 172.5 %all-reduce.3.cloned.1.call-start = ((), (), s32[]{:S(2)}) async-start(), calls=%async_computation.6 | async-start | bytes 262144 | tf_op jit(solution)/shard_map/psum | solution.py:183
  286.5 4.8 collective-permute-start
  288.7 6.4 %collective-permute-start.1 = (f32[8,1,4096]{2,0,1:T(8,128)S(1)}, f32[8,1,4096]{2,0,1:T(8,128)S(1)}, u32[]{:S(2)}, u32[]{:S(2)}) collective-permute-start(f32[8,1,4096]{2,0,1:T(8,128)S(1)} %get-tuple-element.85), channel_id=1, source_target_pairs={{32,0},{64,32},{96,64},{128,96},{160,128},{192,160},{224,192},{33,... | collective-permute-start | bytes 393224 | tf_op jit(solution)/shard_map/ppermute | solution.py:26
  334.7 18.1 %copy-start.5 = (bf16[4,128,128]{2,1,0:T(8,128)(2,1)S(1)}, bf16[4,128,128]{2,1,0:T(8,128)(2,1)}, u32[]{:S(2)}) copy-start(bf16[4,128,128]{2,1,0:T(8,128)(2,1)} %param.13) | copy-start | bytes 393220
  346.0 275.7 %copy-start.1 = (f32[8,4,128,128]{3,2,1,0:T(8,128)S(1)}, f32[8,4,128,128]{3,2,1,0:T(8,128)}, u32[]{:S(2)}) copy-start(f32[8,4,128,128]{3,2,1,0:T(8,128)} %param.14) | copy-start | bytes 6291460
  353.8 239.7 %all-reduce.5.cloned.1.call-start = ((), (), s32[]{:S(2)}) async-start(), calls=%async_computation.7 | async-start | bytes 131072 | tf_op jit(solution)/shard_map/psum | solution.py:186
  484.5 1.5 copy-start.3
Sparse Core Ops, SparseCore 0:
  353.9 104.9 all-reduce.2
  486.1 107.3 all-reduce.4
where the time goes:
time: 633 us; the launch traced here: 629 us
  waiting for transfers between devices  264 us (42%)
  local copies, waits for them, and re-layouts  170 us (27%)
  blocking collectives  73.1 us (12%)
  matrix products  49.3 us (8%)
  other arithmetic  34.9 us (6%)
  starting transfers between devices  20 us (3%)
  between operations  17.3 us (3%)
    unnamed x30, local copies, waits for them, and re-layouts  118 us
    psum x1, waiting for transfers between devices, on_device(): lax.psum(jnp.einsum('krw,jrw->kj', coords, coords, precision=hi), 'chan')  106 us
    psum x1, waiting for transfers between devices, on_device(): sketch = lax.psum(take_sketch(pixels, sketch_rows), 'chan')  105 us
    all_to_all x1, blocking collectives, data_gradient(): lax.all_to_all(inverted, 'facet', split_axis=3, concat_axis=2, tiled=True)  30.5 us
    dot_general x78, matrix products, matmul_hi(): return jnp.dot(first_mat, second_mat, precision=lax.Precision.HIGHEST)  29.9 us
    all_to_all x1, waiting for transfers between devices, data_gradient(): lax.all_to_all(column_spec, 'facet', split_axis=2, concat_axis=3, tiled=T...  28.5 us
    all_to_all x1, blocking collectives, data_gradient(): lax.all_to_all(sky_image, 'facet', split_axis=2, concat_axis=1, tiled=True)  25.4 us
    all_to_all x1, blocking collectives, on_device(): lax.all_to_all(merged, 'chan', split_axis=2, concat_axis=0, tiled=True)  17.2 us
  transfers between devices with their start and end apart: 7, of which 7 were waited for; matrix products, arithmetic and copies ran while one was open for 0% of the time, Pallas kernels for 0%

commit v1 on v0

v1 whole, which is shorter than its diff:
```python
import math

import jax
import jax.numpy as jnp
from jax import lax
from jax.sharding import PartitionSpec as P

SIGN_ITERS = 12
ROOT_ITERS = 14


step_primal = 0.4
smooth_weight = 0.25
step_dual = 0.5
shrink_ratio = 0.25

HI = lax.Precision.HIGHEST


def padded_2(block, sides, width):
    for axis, dim in sides:
        count = lax.axis_size(axis)
        forward = [(i, i + 1) for i in range(count - 1)]
        backward = [(target, source) for source, target in forward]
        low = lax.ppermute(
            lax.slice_in_dim(block, block.shape[dim] - width, None, axis=dim), axis, forward
        )
        high = lax.ppermute(lax.slice_in_dim(block, 0, width, axis=dim), axis, backward)
        block = jnp.concatenate([low, block, high], axis=dim)
    return block


def matmul_hi(first_mat, second_mat):
    return jnp.dot(first_mat, second_mat, precision=HI)


def shrink_matrix(gram_mat):
    order_n = gram_mat.shape[0]
    identity = jnp.eye(order_n, dtype=gram_mat.dtype)
    thresh_sq = shrink_ratio * jnp.trace(gram_mat) / order_n
    shifted = gram_mat - thresh_sq * identity
    signum = shifted / jnp.sqrt(jnp.sum(shifted * shifted))

    def sign_step(turn_no, current):
        return 1.5 * current - 0.5 * matmul_hi(matmul_hi(current, current), current)

    signum = lax.fori_loop(0, SIGN_ITERS, sign_step, signum)
    keeper = 0.5 * (identity + signum)
    floored = 0.5 * (gram_mat + thresh_sq * identity + matmul_hi(shifted, signum))
    scale_c = jnp.sqrt(jnp.sum(floored * floored))

    def root_step(turn_no, state_pair):
        root_iter, inv_iter = state_pair
        step_mat = 0.5 * (3.0 * identity - matmul_hi(inv_iter, root_iter))
        return (matmul_hi(root_iter, step_mat), matmul_hi(step_mat, inv_iter))

    root_iter, inv_iter = lax.fori_loop(0, ROOT_ITERS, root_step, (floored / scale_c, identity))
    inv_root = inv_iter / jnp.sqrt(scale_c)
    return matmul_hi(keeper, identity - jnp.sqrt(thresh_sq) * inv_root)


def phase_of(index, period):
    angle = (2.0 * math.pi / period) * (index % period).astype(jnp.float32)
    return jnp.cos(angle), jnp.sin(angle)


def data_gradient(sky_image, grid_tiles, freq_block, vis_block, vis_all):
    chan_count, row_count, width = sky_image.shape
    block = grid_tiles.shape[2]
    blocks_n = width // block
    all_rows = vis_all.shape[2]
    vb_n = vis_all.shape[3]
    row0 = lax.axis_index("facet") * row_count

    p_idx = lax.broadcasted_iota(jnp.int32, (row_count, all_rows), 1)
    q_idx = lax.broadcasted_iota(jnp.int32, (row_count, all_rows), 0) + row0
    cos_c, sin_c = phase_of(p_idx * q_idx, all_rows)
    col_scale = 1.0 / math.sqrt(all_rows)
    v_re = vis_all[:, 0]
    v_im = vis_all[:, 1]
    u_re = (
        jnp.einsum("qp,cpvm->cvqm", cos_c, v_re, precision=HI)
        - jnp.einsum("qp,cpvm->cvqm", sin_c, v_im, precision=HI)
    ) * col_scale
    u_im = (
        jnp.einsum("qp,cpvm->cvqm", sin_c, v_re, precision=HI)
        + jnp.einsum("qp,cpvm->cvqm", cos_c, v_im, precision=HI)
    ) * col_scale

    n2_idx = lax.broadcasted_iota(jnp.int32, freq_block.shape + (blocks_n,), 2)
    w_cos, w_sin = phase_of(freq_block[:, :, None] * n2_idx, blocks_n)
    n1_idx = lax.broadcasted_iota(jnp.int32, freq_block.shape + (block,), 2)
    t_cos, t_sin = phase_of(freq_block[:, :, None] * n1_idx, width)
    t_cos = t_cos[:, :, None, :]
    t_sin = t_sin[:, :, None, :]
    j_idx = lax.broadcasted_iota(jnp.int32, (block, block), 0)
    m_idx = lax.broadcasted_iota(jnp.int32, (block, block), 1)
    f_cos, f_sin = phase_of(j_idx * m_idx, block)
    row_scale = 1.0 / math.sqrt(width)

    x = sky_image.reshape(chan_count, row_count, blocks_n, block)
    y_re = jnp.einsum("ctn,crnm->ctrm", w_cos, x, precision=HI)
    y_im = -jnp.einsum("ctn,crnm->ctrm", w_sin, x, precision=HI)
    yt_re = y_re * t_cos + y_im * t_sin
    yt_im = y_im * t_cos - y_re * t_sin
    tiles_n = freq_block.shape[1]
    flat = chan_count * tiles_n * row_count
    yt_re = yt_re.reshape(flat, block)
    yt_im = yt_im.reshape(flat, block)
    s_re = (matmul_hi(yt_re, f_cos) + matmul_hi(yt_im, f_sin)) * row_scale
    s_im = (matmul_hi(yt_im, f_cos) - matmul_hi(yt_re, f_sin)) * row_scale
    s_re = s_re.reshape(chan_count, tiles_n, row_count, block)
    s_im = s_im.reshape(chan_count, tiles_n, row_count, block)
    z_re = jnp.einsum("ctrj,ctjm->ctrm", s_re, grid_tiles, precision=HI)
    z_im = jnp.einsum("ctrj,ctjm->ctrm", s_im, grid_tiles, precision=HI)
    place = jax.nn.one_hot(vis_block, vb_n, dtype=jnp.float32)
    r_re = jnp.einsum("ctv,ctrm->cvrm", place, z_re, precision=HI) - u_re
    r_im = jnp.einsum("ctv,ctrm->cvrm", place, z_im, precision=HI) - u_im
    sp_re = jnp.einsum("ctv,cvrm->ctrm", place, r_re, precision=HI)
    sp_im = jnp.einsum("ctv,cvrm->ctrm", place, r_im, precision=HI)
    c_re = jnp.einsum("ctrm,ctjm->ctrj", sp_re, grid_tiles, precision=HI)
    c_im = jnp.einsum("ctrm,ctjm->ctrj", sp_im, grid_tiles, precision=HI)
    c_re = c_re.reshape(flat, block)
    c_im = c_im.reshape(flat, block)
    d_re = (matmul_hi(c_re, f_cos) - matmul_hi(c_im, f_sin)) * row_scale
    d_im = (matmul_hi(c_re, f_sin) + matmul_hi(c_im, f_cos)) * row_scale
    d_re = d_re.reshape(chan_count, tiles_n, row_count, block)
    d_im = d_im.reshape(chan_count, tiles_n, row_count, block)
    dt_re = d_re * t_cos - d_im * t_sin
    dt_im = d_im * t_cos + d_re * t_sin
    grad = jnp.einsum("ctn,ctrm->crnm", w_cos, dt_re, precision=HI) - jnp.einsum(
        "ctn,ctrm->crnm", w_sin, dt_im, precision=HI
    )
    return grad.reshape(chan_count, row_count, width)


def on_device(sky_image, dual_field, sketch_matrix, grid_tiles, freq_block, vis_block, vis_data):
    dual_chan = lax.all_to_all(dual_field, "chan", split_axis=0, concat_axis=2, tiled=True)
    vis_all = lax.all_gather(vis_data, "facet", axis=2, tiled=True)
    padded = padded_2(sky_image, (("facet", 1),), 1)
    gradient = data_gradient(sky_image, grid_tiles, freq_block, vis_block, vis_all)
    smooth = 2.0 * sky_image - padded[:, :-2] - padded[:, 2:]
    new_image = sky_image - step_primal * (gradient + smooth_weight * smooth + dual_chan)
    rest = (1.0 - step_dual) * sky_image - 2.0 * step_dual * step_primal * (
        gradient + smooth_weight * smooth
    )
    rest_pix = lax.all_to_all(rest, "chan", split_axis=2, concat_axis=0, tiled=True)
    pixels = (1.0 - 2.0 * step_dual * step_primal) * dual_field + rest_pix
    chans = pixels.shape[0]
    flat_pix = pixels.reshape(chans, -1)
    sketch_rows = sketch_matrix.astype(jnp.float32).reshape(flat_pix.shape[1], -1)
    rank = sketch_rows.shape[1]
    part = jnp.concatenate(
        [matmul_hi(flat_pix, sketch_rows), jnp.dot(flat_pix, flat_pix.T, precision=HI)], axis=1
    )
    total = lax.psum(part, "chan")
    sketch = total[:, :rank]
    outer = total[:, rank:]
    lower_fac = jnp.linalg.cholesky(matmul_hi(sketch.T, sketch))
    basis_mat = jax.scipy.linalg.solve_triangular(lower_fac, sketch.T, lower=True).T
    gram_mat = matmul_hi(basis_mat.T, matmul_hi(outer, basis_mat))
    shrink = shrink_matrix(gram_mat)
    coords = matmul_hi(basis_mat.T, flat_pix)
    new_dual = flat_pix - matmul_hi(matmul_hi(basis_mat, shrink), coords)
    return (new_image, new_dual.reshape(pixels.shape))


def solution(mesh):
    placed = (
        P("chan", "facet", None),
        P(None, "facet", "chan"),
        P("facet", "chan", None),
        P("chan", None, None, None),
        P("chan", None),
        P("chan", None),
        P("chan", None, "facet", None, None),
    )
    return jax.shard_map(
        on_device,
        mesh=mesh,
        in_specs=placed,
        out_specs=(P("chan", "facet", None), P(None, "facet", "chan")),
        check_vma=False,
    )
```

time: 633 us -> 320 us (0.51)
  waiting for transfers between devices: 264 us -> 128 us
  local copies, waits for them, and re-layouts: 170 us -> 46 us
  blocking collectives: 73.1 us -> 33 us
    psum x2 -> x1, waiting for transfers between devices: 211 us -> 107 us  [on_device(): total = lax.psum(part, 'chan')]
    unnamed x30 -> x18, local copies, waits for them, and re-layouts: 118 us -> 27.3 us
    all_to_all x2 -> x0, waiting for transfers between devices: 44.6 us -> none  [the longest x1 28.5 us: data_gradient(): lax.all_to_all(column_spec, 'facet', split_axis=2, concat_axis=3, tiled=T...]
    all_to_all x3 -> x1, blocking collectives: 73.1 us -> 33 us  [on_device(): lax.all_to_all(rest, 'chan', split_axis=2, concat_axis=0, tiled=True)]
    all_to_all x8 -> x2, local copies, waits for them, and re-layouts: 29.3 us -> 7.23 us  [on_device(): lax.all_to_all(rest, 'chan', split_axis=2, concat_axis=0, tiled=True)]
    all_gather x0 -> x1, waiting for transfers between devices: none -> 20.1 us  [on_device(): vis_all = lax.all_gather(vis_data, 'facet', axis=2, tiled=True)]
    mul x3 -> x0, local copies, waits for them, and re-layouts: 12.6 us -> none  [the longest x2 11.5 us: adjoint_rows(): return rows_out.reshape(row_count, width) * (1.0 / math.sqrt(width))]
    all_to_all x2 -> x0, starting transfers between devices: 7.23 us -> none  [the longest x1 3.73 us: data_gradient(): lax.all_to_all(column_spec, 'facet', split_axis=2, concat_axis=3, tiled=T...]
  transfers between devices with their start and end apart: 7 -> 5, of which waited for: 7 -> 2; matrix products, arithmetic and copies ran while one was open for 0% -> 9% of each run, Pallas kernels for 0% -> 0%
where the time goes in v1:
time: 320 us; the launch traced here: 314 us
  waiting for transfers between devices  128 us (40%)
  local copies, waits for them, and re-layouts  46 us (14%)
  matrix products  44.8 us (14%)
  blocking collectives  33 us (10%)
  other arithmetic  30.3 us (9%)
  between operations  16.8 us (5%)
  starting transfers between devices  14.6 us (5%)
    psum x1, waiting for transfers between devices, on_device(): total = lax.psum(part, 'chan')  107 us
    all_to_all x1, blocking collectives, on_device(): lax.all_to_all(rest, 'chan', split_axis=2, concat_axis=0, tiled=True)  33 us
    unnamed x18, local copies, waits for them, and re-layouts  27.3 us
    dot_general x83, matrix products, matmul_hi(): return jnp.dot(first_mat, second_mat, precision=HI)  25.7 us
    all_gather x1, waiting for transfers between devices, on_device(): vis_all = lax.all_gather(vis_data, 'facet', axis=2, tiled=True)  20.1 us
    another operation x3, other arithmetic, on_device(): lower_fac = jnp.linalg.cholesky(matmul_hi(sketch.T, sketch))  12.4 us
    another operation x2, other arithmetic, on_device(): jax.scipy.linalg.solve_triangular(lower_fac, sketch.T, lower=True)  10.5 us
    all_to_all x1, starting transfers between devices, on_device(): lax.all_to_all(dual_field, 'chan', split_axis=0, concat_axis=2, tiled=True)  8.2 us
  transfers between devices with their start and end apart: 5, of which 2 were waited for; matrix products, arithmetic and copies ran while one was open for 9% of the time, Pallas kernels for 0%

profile of v1, /device:TPU:1, one launch (start us, length us, event | category | flops | bytes accessed | tf_op | source)
XLA Modules:
  0.0 314.2 jit_solution(2207416730779569240)
XLA Ops:
  7.2 1.5 copy.158
  8.7 0.7 fusion.201
  9.4 1.3 collective-permute-start.1
  10.7 5.0 %collective-permute-start = (f32[8,1,4096]{2,0,1:T(8,128)}, f32[8,1,4096]{2,0,1:T(8,128)S(1)}, u32[]{:S(2)}, u32[]{:S(2)}) collective-permute-start(f32[8,1,4096]{2,0,1:T(8,128)} %get-tuple-element.81), channel_id=1, source_target_pairs={{0,32},{32,64},{64,96},{96,128},{128,160},{160,192},{192,224},{1,3... | collective-permute-start | bytes 393224 | tf_op jit(solution)/shard_map/ppermute | solution.py:25
  15.7 1.6 copy.132
  17.4 8.2 %all-to-all-start = ((f32[256,4,128]{2,1,0:T(4,128)}), f32[256,4,128]{2,1,0:T(4,128)}, u32[]{:S(2)}, u32[]{:S(2)}) async-start(f32[256,4,128]{2,1,0:T(4,128)} %param.12), calls=%async_computation | async-start | bytes 1048576 | tf_op jit(solution)/shard_map/all_to_all | solution.py:138
  25.7 1.4 reshape.74
  27.4 0.6 convolution_negate_fusion
  27.9 0.6 multiply_subtract_fusion.1
  28.5 0.5 fusion.85
  29.1 0.5 fusion.81
  29.6 0.5 fusion.9
  30.0 1.9 fusion.204
  31.9 0.3 fusion.49
  32.2 0.5 fusion.8
  32.7 1.9 fusion.205
  34.6 0.3 fusion.42
  34.9 20.1 %all-gather.2.cloned.1.call-done = f32[8,2,32,4,128]{4,0,3,1,2:T(8,128)} async-done(((f32[8,2,4,4,128]{4,0,3,1,2:T(8,128)}), f32[8,2,32,4,128]{4,0,3,1,2:T(8,128)}) %all-gather.2.cloned.1.call-update) | async-done | bytes 1048592 | tf_op jit(solution)/shard_map/all_gather | solution.py:139
  55.1 1.3 fusion.200
  56.3 0.7 fusion.21
  57.0 0.7 fusion.20
  57.7 0.7 fusion.19
  58.4 0.7 fusion.18
  59.4 3.6 %fusion.44 = f32[8,4,4,128]{3,2,1,0:T(4,128)S(1)} fusion(f32[8,4,128,128]{3,2,1,0:T(8,128)S(1)} %copy-done, f32[8,4,4,128]{3,1,2,0:T(4,128)S(1)} %fusion.46), kind=kOutput, calls=%fused_computation.75 | convolution fusion | flops 25165824 | bytes 2228224 | tf_op jit(solution)/shard_map/ctrm,ctjm->ctrj/dot_general | solution.py:121
  63.0 0.5 fusion.87
  63.5 0.5 fusion.83
  64.3 3.4 %fusion.37 = f32[8,4,4,128]{3,2,1,0:T(4,128)S(1)} fusion(f32[8,4,128,128]{3,2,1,0:T(8,128)S(1)} %copy-done, f32[8,4,4,128]{3,1,2,0:T(4,128)S(1)} %fusion.39), kind=kOutput, calls=%fused_computation.67 | convolution fusion | flops 25165824 | bytes 2228224 | tf_op jit(solution)/shard_map/ctrm,ctjm->ctrj/dot_general | solution.py:122
  67.7 0.5 fusion.6
  68.1 0.5 fusion.7
  68.6 0.8 fusion.62
  69.4 0.8 fusion.4
  70.2 2.5 multiply_subtract_fusion
  72.7 6.7 %copy.160 = f32[8,4,4096]{0,1,2:T(4,128)} copy(f32[8,4,4096]{2,0,1:T(8,128)} %get-tuple-element.77) | data formatting | bytes 1048576 | tf_op jit(solution)/shard_map/sub | solution.py:144
  79.4 11.4 %reshape.95 = f32[32,1,4096]{2,1,0:T(1,128)S(1)} reshape(f32[4096,4,8]{2,1,0:T(4,128)} %bitcast.164) | data formatting | bytes 1048576
  90.9 33.0 %all_to_all.36 = f32[32,1,4096]{2,1,0:T(1,128)S(1)} all-to-all(f32[32,1,4096]{2,1,0:T(1,128)S(1)} %reshape.95), channel_id=1, replica_groups=mesh['facet'=8,'chan'=32] {'chan'}, dimensions={0} | all-to-all | bytes 1048576 | tf_op jit(solution)/shard_map/all_to_all | solution.py:147
  123.9 0.5 broadcast.237
  124.4 1.9 reduce.6
  126.3 11.3 %reshape.96 = f32[4096,4,8]{2,1,0:T(4,128)} reshape(f32[32,4096]{1,0:T(8,128)S(1)} %reduce.6) | data formatting | bytes 1048576
  137.6 6.7 %copy.161 = f32[32,8,4,128]{3,2,1,0:T(4,128)S(1)} copy(f32[32,8,4,128]{1,2,3,0:T(4,128)} %bitcast.165) | data formatting | bytes 1048576 | tf_op jit(solution)/shard_map/all_to_all | solution.py:147
  144.3 1.3 bitcast_add_fusion.1
  145.6 0.6 convolution_bitcast_fusion.1
  146.2 0.5 convolution_bitcast_fusion.2
  146.7 0.8 pad_maximum_fusion.2
  147.5 1.1 copy.168
  148.7 107.5 %all-reduce.2.cloned.1.call-done = f32[256,384]{0,1:T(8,128)} async-done(((f32[256,384]{0,1:T(8,128)}), f32[256,384]{0,1:T(8,128)}) %all-reduce.2.cloned.1.call-update) | async-done | bytes 393232 | tf_op jit(solution)/shard_map/psum | solution.py:156
  256.1 1.3 fusion.29
  257.5 11.7 %cholesky.22 = f32[128,128]{1,0:T(8,128)S(1)} custom-call(f32[128,128]{1,0:T(8,128)S(1)} %fusion.36), custom_call_target="Cholesky" | custom-call | tf_op jit(solution)/shard_map/jit(cholesky)/cholesky | solution.py:159
  269.2 0.6 compare_reduce_fusion
  269.9 0.7 fusion.31
  270.5 9.8 %custom-call.7 = f32[1,128,128]{1,2,0:T(8,128)S(1)} custom-call(f32[1,128,128]{2,1,0:T(8,128)S(1)} %fusion.31), custom_call_target="InvertDiagBlocksLowerTriangular" | custom-call | tf_op jit(solution)/shard_map/jit(_solve_triangular)/triangular_solve | solution.py:160
  280.4 1.2 fusion.27
  281.6 1.5 fusion.25
  283.1 0.9 select_reduce_fusion
  284.7 0.6 multiply_reduce_fusion.1
  286.0 5.4 %while.23 = (s32[]{:T(128)}, f32[128,128]{1,0:T(8,128)S(1)}, s32[]{:T(128)}) while((s32[]{:T(128)}, f32[128,128]{1,0:T(8,128)S(1)}, s32[]{:T(128)}) %tuple.53), condition=%wide.region_6.7_spmd, body=%wide.region_5.6_spmd.sunk | while | flops 50380800 | bytes 458797 | solution.py:47
  291.5 0.8 multiply_reduce_fusion
  293.1 11.5 %while.24 = (s32[]{:T(128)}, f32[128,128]{0,1:T(8,128)S(1)}, f32[128,128]{1,0:T(8,128)S(1)}, s32[]{:T(128)}) while((s32[]{:T(128)}, f32[128,128]{0,1:T(8,128)S(1)}, f32[128,128]{1,0:T(8,128)S(1)}, s32[]{:T(128)}) %tuple.56), condition=%wide.region_9.10_spmd.clone, body=%wide.region_8.9_spmd.clone.sunk | while | flops 75563008 | bytes 852021 | solution.py:57
  295.1 0.3 convolution_bitcast_fusion.4
  295.9 0.3 convolution_bitcast_fusion.4
  296.7 0.3 convolution_bitcast_fusion.4
  304.8 0.4 fusion.206
  305.2 0.4 fusion.10
  305.7 0.6 convolution_subtract_fusion.2
  306.2 1.0 reshape.85
  (138 shorter events, 16.6 us)
Async XLA Ops:
  7.2 22.9 %copy-start = (f32[8,4,128,128]{3,2,1,0:T(8,128)S(1)}, f32[8,4,128,128]{3,2,1,0:T(8,128)}, u32[]{:S(2)}) copy-start(f32[8,4,128,128]{3,2,1,0:T(8,128)} %param.14) | copy-start | bytes 6291460
  7.2 19.9 %copy-start.3 = (s32[8,4]{0,1:T(4,128)S(1)}, s32[8,4]{0,1:T(4,128)}, u32[]{:S(2)}) copy-start(s32[8,4]{0,1:T(4,128)} %param.15) | copy-start | bytes 388
  7.2 47.9 %all-gather.2.cloned.1.call-start = ((), (), s32[]{:S(2)}) async-start(), calls=%async_computation.2 | async-start | bytes 1179648 | tf_op jit(solution)/shard_map/all_gather | solution.py:139
  9.4 60.7 %collective-permute-start.1 = (f32[8,1,4096]{2,0,1:T(8,128)}, f32[8,1,4096]{2,0,1:T(8,128)S(1)}, u32[]{:S(2)}, u32[]{:S(2)}) collective-permute-start(f32[8,1,4096]{2,0,1:T(8,128)} %get-tuple-element.82), channel_id=1, source_target_pairs={{32,0},{64,32},{96,64},{128,96},{160,128},{192,160},{224,192},{33,... | collective-permute-start | bytes 393224 | tf_op jit(solution)/shard_map/ppermute | solution.py:28
  10.7 59.5 %collective-permute-start = (f32[8,1,4096]{2,0,1:T(8,128)}, f32[8,1,4096]{2,0,1:T(8,128)S(1)}, u32[]{:S(2)}, u32[]{:S(2)}) collective-permute-start(f32[8,1,4096]{2,0,1:T(8,128)} %get-tuple-element.81), channel_id=1, source_target_pairs={{0,32},{32,64},{64,96},{96,128},{128,160},{160,192},{192,224},{1,3... | collective-permute-start | bytes 393224 | tf_op jit(solution)/shard_map/ppermute | solution.py:25
  17.4 11.7 %copy-start.4 = (s32[8,4]{0,1:T(4,128)S(1)}, s32[8,4]{0,1:T(4,128)}, u32[]{:S(2)}) copy-start(s32[8,4]{0,1:T(4,128)} %param.16) | copy-start | bytes 388
  17.4 52.8 %all-to-all-start = ((f32[256,4,128]{2,1,0:T(4,128)}), f32[256,4,128]{2,1,0:T(4,128)}, u32[]{:S(2)}, u32[]{:S(2)}) async-start(f32[256,4,128]{2,1,0:T(4,128)} %param.12), calls=%async_computation | async-start | bytes 1048576 | tf_op jit(solution)/shard_map/all_to_all | solution.py:138
  25.6 230.5 %all-reduce.2.cloned.1.call-start = ((), (), s32[]{:S(2)}) async-start(), calls=%async_computation.3 | async-start | bytes 786432 | tf_op jit(solution)/shard_map/psum | solution.py:156
  144.3 1.9 copy-start.2
  145.6 1.9 copy-start.1
Sparse Core Ops, SparseCore 0:
  17.5 37.4 all-gather.1
  147.6 108.4 all-reduce.1
